TPU v7x, 32 devices: a whole 2x2x4 slice. The times are simulated.
32 devices in a mesh: groups: 2 (over y), blk: 4 (over z), pool: 4 (over x, core).
Axes of the slice: x: 2, y: 2, z: 4, core: 2. Of those that a mesh axis runs over, the one named last changes fastest.
Arguments:
- q_new: bfloat16 [1024, 8192], P(('groups', 'blk'), 'pool'), parts along dimension 0, may hold values from -64 to 64
- kv_new: bfloat16 [1024, 8, 256], P(('groups', 'blk'), 'pool'), parts along dimension 0, may hold values from -7 to 7
- kv_cache: bfloat16 [256, 8, 128, 256], P(('groups', 'blk'), 'pool'), parts along dimension 0, may hold values from -4.5 to 4.5
- page_table: int32 [16], P('groups'), parts along dimension 0, may hold values from 0 to 127, as said below
- block_offsets: int32 [8], P('groups'), parts along dimension 0, may hold values from 0 to 3, each once
Outputs:
- attended: bfloat16 [1024, 8192], P(('groups', 'blk'), 'pool'), parts along dimension 0
There are 2 independent parts, one for each index of `groups`. A program takes and returns all parts, laid end to end along the dimension named above; each array names one. Nothing has to cross between parts.
Inputs may be any that keep to these rules, and one draw needn't show every extreme that they name: `page_table`: distinct slots; slot s lies on blk index s // 32; at most 4 entries lie on the slots of one blk index, and exactly 4 on some blk index.
All inputs are finite; a program needn't handle non-finite values.
Results may differ from a plain program's by a relative error of at most 0.0045.
Values may be sent and summed in bfloat16 or wider, within the bound.
No kernel may reach another device: no remote copies, remote signals or barrier semaphores. Data moves between devices by JAX's collectives and lax.ppermute only.
A program may use at most 64 MiB of HBM per device.

v0:
```python
import math
import jax
import jax.numpy as jnp
from jax import lax
from jax.sharding import PartitionSpec as P

CAP = 4


def attend(running, queries, keys, values, visible, head_size):
    maxima, totals, summed = running
    score_scale = 1.0 / math.sqrt(head_size)
    scores = (
        jnp.einsum("gqd,gkd->gqk", queries, keys, preferred_element_type=jnp.float32) * score_scale
    )
    scores = jnp.where(visible, scores, -1e30)
    row_top = jnp.maximum(maxima, jnp.max(scores, axis=2))
    factor = jnp.exp(maxima - row_top)
    weights = jnp.where(visible, jnp.exp(scores - row_top[..., None]), 0.0)
    totals = totals * factor + jnp.sum(weights, axis=2)
    summed = summed * factor[..., None] + jnp.einsum(
        "gqk,gkd->gqd", weights.astype(jnp.bfloat16), values, preferred_element_type=jnp.float32
    )
    return (row_top, totals, summed)


def local(q_new, kv_new, kv_cache, page_table, block_offsets):
    q_rows = q_new.shape[0]
    kv_heads = kv_new.shape[1]
    head_size = kv_new.shape[2] // 2
    group_size = q_new.shape[1] // (head_size * kv_heads)
    slots_dev = kv_cache.shape[0]
    page_len = kv_cache.shape[2]
    npages = page_table.shape[0]
    blocks = lax.axis_size("blk")
    myself = lax.axis_index("blk")
    pg = -(-npages // blocks)
    block_ids = jnp.arange(blocks, dtype=jnp.int32)
    my_offset = jnp.sum(jnp.where(block_ids == myself, block_offsets, 0))
    query_pos = jnp.tile(my_offset * q_rows + jnp.arange(q_rows, dtype=jnp.int32), group_size)
    queries = (
        q_new.reshape(q_rows, kv_heads, group_size, head_size)
        .transpose(1, 2, 0, 3)
        .reshape(kv_heads, group_size * q_rows, head_size)
    )
    query_span = group_size * q_rows
    page_owner = page_table // slots_dev
    owned = page_owner == myself
    page_rank = jnp.cumsum(owned.astype(jnp.int32)) - 1
    local_slot = page_table % slots_dev
    counts = jnp.sum((page_owner[None, :] == block_ids[:, None]).astype(jnp.int32), axis=1)
    per_peer = (CAP + blocks - 1) // blocks
    starts = jnp.cumsum(counts) - counts
    my_start = jnp.sum(jnp.where(block_ids == myself, starts, 0))
    peer_slots = jnp.arange(per_peer, dtype=jnp.int32)[None, :]
    wanted = (block_ids[:, None] - my_start) % blocks + peer_slots * blocks
    picked = owned[None, None, :] & (page_rank[None, None, :] == wanted[..., None])
    chosen = jnp.sum(jnp.where(picked, local_slot[None, None, :], 0), axis=2).reshape(-1)
    sent_pages = kv_cache[chosen].reshape(blocks, per_peer, kv_heads, page_len, 2 * head_size)
    sent_pages = sent_pages.transpose(0, 2, 1, 3, 4).reshape(
        blocks, kv_heads, per_peer * page_len, 2 * head_size
    )
    own_rows = jnp.broadcast_to(
        kv_new.transpose(1, 0, 2)[None], (blocks, kv_heads, q_rows, 2 * head_size)
    )
    payload = jnp.concatenate([sent_pages, own_rows], axis=2)
    received = lax.all_to_all(payload, "blk", split_axis=0, concat_axis=0, tiled=True)
    page_part = received[:, :, : per_peer * page_len]
    page_part = page_part.reshape(blocks, kv_heads, per_peer, page_len, 2 * head_size)
    page_part = page_part.transpose(0, 2, 1, 3, 4).reshape(
        blocks * per_peer, kv_heads, page_len, 2 * head_size
    )
    arriving = (myself - starts[:, None]) % blocks + peer_slots * blocks
    present = (arriving < counts[:, None]).reshape(-1)
    order_rank = jnp.cumsum(present.astype(jnp.int32)) - 1
    choose = present[None, :] & (order_rank[None, :] == jnp.arange(pg, dtype=jnp.int32)[:, None])
    positions = jnp.sum(
        jnp.where(choose, jnp.arange(blocks * per_peer, dtype=jnp.int32)[None, :], 0), axis=1
    )
    compact = page_part[positions]
    compact_valid = jnp.arange(pg, dtype=jnp.int32) * blocks + myself < npages
    gathered = lax.all_gather(compact, "blk", axis=0, tiled=True)
    gathered_valid = (
        jnp.arange(pg, dtype=jnp.int32)[None, :] * blocks + block_ids[:, None] < npages
    ).reshape(-1)
    new_rows = received[:, :, per_peer * page_len :]
    new_rows = new_rows.transpose(1, 0, 2, 3).reshape(kv_heads, blocks * q_rows, 2 * head_size)
    own_pages = compact.transpose(1, 0, 2, 3).reshape(kv_heads, pg * page_len, 2 * head_size)
    entries_a = jnp.concatenate([new_rows, own_pages], axis=1)
    row_source = jnp.repeat(block_ids, q_rows)
    key_pos = jnp.sum(
        jnp.where(row_source[:, None] == block_ids[None, :], block_offsets[None, :], 0), axis=1
    ) * q_rows + jnp.tile(jnp.arange(q_rows, dtype=jnp.int32), blocks)
    visible_new = key_pos[None, :] <= query_pos[:, None]
    visible_own = jnp.broadcast_to(
        jnp.repeat(compact_valid, page_len)[None, :], (query_span, pg * page_len)
    )
    visible_a = jnp.concatenate([visible_new, visible_own], axis=1)[None]
    running = (
        jnp.full((kv_heads, query_span), -1e30, jnp.float32),
        jnp.zeros((kv_heads, query_span), jnp.float32),
        jnp.zeros((kv_heads, query_span, head_size), jnp.float32),
    )
    running = attend(
        running,
        queries,
        entries_a[..., :head_size],
        entries_a[..., head_size:],
        visible_a,
        head_size,
    )
    page_block = jnp.repeat(block_ids, pg)
    use_page = gathered_valid & (page_block != myself)
    entries_b = gathered.transpose(1, 0, 2, 3).reshape(
        kv_heads, blocks * pg * page_len, 2 * head_size
    )
    visible_b = jnp.repeat(use_page, page_len)[None, None, :]
    running = attend(
        running,
        queries,
        entries_b[..., :head_size],
        entries_b[..., head_size:],
        visible_b,
        head_size,
    )
    maxima, totals, summed = running
    attended = (summed / totals[..., None]).astype(jnp.bfloat16)
    attended = attended.reshape(kv_heads, group_size, q_rows, head_size).transpose(2, 0, 1, 3)
    return attended.reshape(q_rows, kv_heads * group_size * head_size)


def solution(mesh):
    return jax.shard_map(
        local,
        mesh=mesh,
        in_specs=(
            P(("groups", "blk"), "pool"),
            P(("groups", "blk"), "pool", None),
            P(("groups", "blk"), "pool", None, None),
            P("groups"),
            P("groups"),
        ),
        out_specs=P(("groups", "blk"), "pool"),
        check_vma=False,
    )
```

profile of v0, /device:TPU:0, one launch (start us, length us, event | category | flops | bytes accessed | tf_op | source)
XLA Modules:
  0.0 97.5 jit_solution(11759745901006424764)
XLA Ops:
  6.5 0.0 copy-start.1
  6.5 0.0 copy-start
  6.5 0.7 and_select_fusion.3
  7.3 0.7 convert_bitcast_fusion
  7.9 0.2 reduce-window.21
  8.1 0.1 convert_reduce_fusion
  8.2 0.2 reduce-window.22
  8.4 1.4 %fusion.35 = (s32[]{:T(128)}, s32[]{:T(128)}) fusion(s32[4]{0:T(128)} %param.9, s32[]{:T(128)S(6)} %axis_index.15, s32[4]{0:T(128)S(1)} %convert_reduce_fusion, s32[4,1]{0,1:T(1,128)S(1)} %reduce-window.22), kind=kLoop, calls=%fused_computation.78 | loop fusion | flops 22 | bytes 60 | tf_op jit(solution)/shard_map/reduce_sum | solution.py:39
  9.8 0.7 and_select_fusion.4
  10.5 0.2 select_reduce_fusion.1
  10.7 0.9 copy.22
  11.6 2.8 %gather_fusion = bf16[4,2,128,256]{3,2,1,0:T(8,128)(2,1)S(1)} fusion(bf16[32,2,128,256]{3,2,1,0:T(8,128)(2,1)} %param.7, s32[1024]{0:T(1024)S(1)} %pad_clamp_fusion.1), kind=kCustom, calls=%fused_computation | custom fusion | bytes 1048592 | tf_op jit(solution)/shard_map/gather | solution.py:59
  14.4 1.1 %pad_maximum_fusion = bf16[4,2,256,256]{3,2,1,0:T(8,128)(2,1)} fusion(bf16[4,2,128,256]{3,2,1,0:T(8,128)(2,1)S(1)} %broadcast_in_dim.150, bf16[4,2,128,256]{3,2,1,0:T(8,128)(2,1)S(1)} %gather_fusion), kind=kLoop, calls=%fused_computation.23 | loop fusion | flops 2097152 | bytes 2097152 | tf_op jit(solution)/shard_map/concatenate | solution.py:66
  15.5 6.3 %all-to-all-start = ((bf16[4,2,256,256]{3,2,1,0:T(8,128)(2,1)}), bf16[4,2,256,256]{3,2,1,0:T(8,128)(2,1)S(1)}, u32[]{:S(2)}, u32[]{:S(2)}) async-start(bf16[4,2,256,256]{3,2,1,0:T(8,128)(2,1)} %pad_maximum_fusion), calls=%async_computation | async-start | bytes 2097152 | tf_op jit(solution)/shard_map/all_to_all | solution.py:67
  21.8 0.0 all-gather.3.cloned.1.call-start
  21.9 0.1 and.99
  21.9 0.2 reduce-window.23
  22.1 0.0 copy-done
  22.1 0.1 copy.32
  22.2 0.1 copy.25
  22.4 0.1 broadcast_bitcast_fusion.2
  23.2 0.1 fusion.33
  23.3 0.0 copy-done.1
  23.3 0.1 select_reduce_fusion
  23.4 24.1 %all-to-all-done = bf16[4,2,256,256]{3,2,1,0:T(8,128)(2,1)S(1)} async-done(((bf16[4,2,256,256]{3,2,1,0:T(8,128)(2,1)}), bf16[4,2,256,256]{3,2,1,0:T(8,128)(2,1)S(1)}, u32[]{:S(2)}, u32[]{:S(2)}) %all-to-all-start) | async-done | bytes 1048608 | tf_op jit(solution)/shard_map/all_to_all | solution.py:67
  47.6 0.1 fusion.51
  47.7 1.3 %gather_fusion.1 = bf16[2,2,128,256]{3,2,1,0:T(8,128)(2,1)} fusion(bf16[4,2,128,256]{3,2,1,0:T(8,128)(2,1)S(1)} %get-tuple-element.10, s32[1024]{0:T(1024)S(1)} %pad_clamp_fusion), kind=kCustom, calls=%fused_computation.1 | custom fusion | bytes 524296 | tf_op jit(solution)/shard_map/gather | solution.py:80
  48.9 0.0 all-gather.3.cloned.1.call-update
  48.9 0.1 broadcast_bitcast_fusion.1
  49.0 0.4 broadcast_compare_fusion
  49.4 0.4 pad_add_fusion
  49.8 1.0 copy.24
  50.8 4.0 %fusion.4 = (f32[2,1024]{1,0:T(2,128)S(1)}, f32[2,768,1024]{2,1,0:T(8,128)}) fusion(pred[1024,768]{0,1:T(8,128)(4,1)S(1)} %pad_add_fusion, bf16[2,1024,128]{2,1,0:T(8,128)(2,1)S(1)} %bitcast.92, bf16[2,512,256]{2,1,0:T(8,128)(2,1)S(1)} %bitcast.98, bf16[2,256,256]{2,1,0:T(8,128)(2,1)S(1)} %bitcast.101), kind=kOutput, calls=%fused_computation.11 | convolution fusion | flops 408156160 | bytes 8396800 | tf_op jit(solution)/shard_map/gqd,gkd->gqk/dot_general | solution.py:14
  54.9 21.3 %all-gather.3.cloned.1.call-done = bf16[8,2,128,256]{3,2,1,0:T(8,128)(2,1)} async-done(((bf16[2,2,128,256]{3,2,1,0:T(8,128)(2,1)}), bf16[8,2,128,256]{3,2,1,0:T(8,128)(2,1)}) %all-gather.3.cloned.1.call-update) | async-done | bytes 1048592 | tf_op jit(solution)/shard_map/all_gather | solution.py:82
  76.1 1.3 %copy.27 = bf16[2,8,128,256]{3,2,1,0:T(8,128)(2,1)S(1)} copy(bf16[2,8,128,256]{3,2,0,1:T(8,128)(2,1)} %bitcast.96) | data formatting | bytes 2097152 | tf_op jit(solution)/shard_map/transpose | solution.py:114
  77.4 0.0 slice-start
  77.4 0.0 slice-start.1
  77.5 1.9 %bitcast_reduce_fusion = (f32[2,1024]{1,0:T(2,128)S(1)}, f32[2,1024,1024]{2,1,0:T(8,128)S(1)}) fusion(pred[1024]{0:T(1024)(128)(4,1)S(1)} %broadcast_bitcast_fusion.1, bf16[2,1024,128]{2,1,0:T(8,128)(2,1)S(1)} %bitcast.93, bf16[2,1024,256]{2,1,0:T(8,128)(2,1)S(1)} %bitcast.89), kind=kOutput, calls=%fused_computation.3 | convolution fusion | flops 543160320 | bytes 9446400 | tf_op jit(solution)/shard_map/gqd,gkd->gqk/dot_general | solution.py:14
  79.4 2.5 %fusion.2 = f32[2,1024]{1,0:T(2,128)S(1)} fusion(f32[2,1024,1024]{2,1,0:T(8,128)S(1)} %get-tuple-element.18, f32[2,1024]{1,0:T(2,128)S(1)} %get-tuple-element.13, pred[1024]{0:T(1024)(128)(4,1)S(1)} %broadcast_bitcast_fusion.1), kind=kLoop, calls=%fused_computation.9 | loop fusion | flops 10483712 | bytes 8406016 | tf_op jit(solution)/shard_map/reduce_sum | solution.py:20
  81.9 0.0 slice-done
  81.9 0.0 slice-done.1
  81.9 1.7 %fusion.5 = f32[2,1024]{1,0:T(2,128)S(1)} fusion(f32[2,768,1024]{2,1,0:T(8,128)S(1)} %bitcast.88, f32[2,1024]{1,0:T(2,128)S(1)} %get-tuple-element.14, pred[1024,768]{0,1:T(8,128)(4,1)S(1)} %pad_add_fusion), kind=kLoop, calls=%fused_computation.12 | loop fusion | flops 7862272 | bytes 7094272 | tf_op jit(solution)/shard_map/reduce_sum | solution.py:20
  83.6 2.8 %fusion.20 = f32[2,1024,128]{2,1,0:T(8,128)S(1)} fusion(f32[2,768,1024]{2,1,0:T(8,128)S(1)} %bitcast.88, f32[2,1024]{1,0:T(2,128)S(1)} %get-tuple-element.14, pred[1024,768]{0,1:T(8,128)(4,1)S(1)} %pad_add_fusion, f32[2,1024]{1,0:T(2,128)S(1)} %get-tuple-element.6, f32[2,1024]{1,0:T(2,128)S(1)} %get-tuple-element.12, ...), kind=kOutput, calls=%fused_computation.22 | convolution fusion | flops 411828224 | bytes 8937472 | tf_op jit(solution)/shard_map/gqk,gkd->gqd/dot_general | solution.py:21
  86.4 3.0 %divide_convert_fusion = bf16[2,1024,128]{2,1,0:T(8,128)(2,1)S(1)} fusion(f32[2,1024,128]{2,1,0:T(8,128)S(1)} %fusion.20, f32[2,1024,1024]{2,1,0:T(8,128)S(1)} %get-tuple-element.18, f32[2,1024]{1,0:T(2,128)S(1)} %get-tuple-element.13, pred[1024]{0:T(1024)(128)(4,1)S(1)} %broadcast_bitcast_fusion.1, bf16[2,1024,256]{2,1,0:T(8,128)(2,1)S(1)} %bitcast.90, ...), kind=kOutput, calls=%fused_computation.24 | convolution fusion | flops 548143104 | bytes 10504192 | tf_op jit(solution)/shard_map/gqk,gkd->gqd/dot_general | solution.py:21
  89.4 0.3 copy.29
  89.8 0.9 copy.35
  (21 shorter events, 0.2 us)
Async XLA Ops:
  6.5 16.8 %copy-start.1 = (s32[4]{0:T(128)S(1)}, s32[4]{0:T(128)}, u32[]{:S(2)}) copy-start(s32[4]{0:T(128)} %param.9) | copy-start | bytes 52
  6.5 15.6 %copy-start = (bf16[128,2048]{1,0:T(8,128)(2,1)S(1)}, bf16[128,2048]{1,0:T(8,128)(2,1)}, u32[]{:S(2)}) copy-start(bf16[128,2048]{1,0:T(8,128)(2,1)} %param.5) | copy-start | bytes 1572868
  15.5 32.0 %all-to-all-start = ((bf16[4,2,256,256]{3,2,1,0:T(8,128)(2,1)}), bf16[4,2,256,256]{3,2,1,0:T(8,128)(2,1)S(1)}, u32[]{:S(2)}, u32[]{:S(2)}) async-start(bf16[4,2,256,256]{3,2,1,0:T(8,128)(2,1)} %pad_maximum_fusion), calls=%async_computation | async-start | bytes 2097152 | tf_op jit(solution)/shard_map/all_to_all | solution.py:67
  21.8 54.3 %all-gather.3.cloned.1.call-start = ((), (), s32[]{:S(2)}) async-start(), calls=%async_computation.1 | async-start | bytes 1310720 | tf_op jit(solution)/shard_map/all_gather | solution.py:82
  77.4 4.5 %slice-start = ((s8[6291456]{0:T(1024)(128)(4,1)}), s8[4194304]{0:T(1024)(128)(4,1)S(1)}, s32[]{:S(2)}) async-start(s8[6291456]{0:T(1024)(128)(4,1)} %bitcast.87), calls=%async_computation.2 | async-start | bytes 8388608
  77.4 4.5 %slice-start.1 = ((s8[6291456]{0:T(1024)(128)(4,1)}), s8[2097152]{0:T(1024)(128)(4,1)S(1)}, s32[]{:S(2)}) async-start(s8[6291456]{0:T(1024)(128)(4,1)} %bitcast.87), calls=%async_computation.3 | async-start | bytes 4194304
Sparse Core Ops, SparseCore 0:
  49.1 27.0 all-gather.2
where the time goes:
time: 97.9 us; the launch traced here: 97.5 us
  waiting for transfers between devices  45.4 us (46%)
  between operations  14.3 us (15%)
  matrix products  11.7 us (12%)
  other arithmetic  10.6 us (11%)
  local copies, waits for them, and re-layouts  9.17 us (9%)
  starting transfers between devices  6.32 us (6%)
    all_to_all x1, waiting for transfers between devices, local(): lax.all_to_all(payload, 'blk', split_axis=0, concat_axis=0, tiled=True)  24.1 us
    all_gather x1, waiting for transfers between devices, local(): gathered = lax.all_gather(compact, 'blk', axis=0, tiled=True)  21.3 us
    all_to_all x1, starting transfers between devices, local(): lax.all_to_all(payload, 'blk', split_axis=0, concat_axis=0, tiled=True)  6.32 us
    dot_general x2, matrix products, attend(): jnp.einsum('gqd,gkd->gqk', queries, keys, preferred_element_type=jnp.floa...  5.92 us
    dot_general x2, matrix products, attend(): jnp.einsum('gqk,gkd->gqd', weights.astype(jnp.bfloat16), values, preferre...  5.81 us
    reduce_sum x2, other arithmetic, attend(): totals = totals * factor + jnp.sum(weights, axis=2)  4.16 us
    gather x1, local copies, waits for them, and re-layouts, local(): kv_cache[chosen]  2.77 us
  transfers between devices with their start and end apart: 2, of which 2 were waited for; matrix products, arithmetic and copies ran while one was open for 7% of the time, Pallas kernels for 0%

commit v1 on v0

--- a/solution.py
+++ b/solution.py
@@ -79,7 +79,24 @@
     )
     compact = page_part[positions]
     compact_valid = jnp.arange(pg, dtype=jnp.int32) * blocks + myself < npages
-    gathered = lax.all_gather(compact, "blk", axis=0, tiled=True)
+    z1, then, f_now = (lax.axis_size("blk"), lax.axis_index("blk"), compact.shape[0])
+    seen = [q * z1 if dd == 0 else q for dd, q in enumerate(compact.shape)]
+    small = k_now = compact
+    gathered = lax.dynamic_update_slice_in_dim(
+        jnp.zeros(seen, compact.dtype), compact, then * f_now, axis=0
+    )
+    for jj in [*range(1, z1 // 2 + 1)]:
+        small = lax.ppermute(small, axis_name="blk", perm=[(dd, (dd + 1) % z1) for dd in range(z1)])
+        gathered = lax.dynamic_update_slice_in_dim(
+            gathered, small, (then - jj) % z1 * f_now, axis=0
+        )
+        if 2 * jj < z1:
+            k_now = lax.ppermute(
+                k_now, axis_name="blk", perm=[(dd, (dd - 1) % z1) for dd in range(z1)]
+            )
+            gathered = lax.dynamic_update_slice_in_dim(
+                gathered, k_now, (then + jj) % z1 * f_now, axis=0
+            )
     gathered_valid = (
         jnp.arange(pg, dtype=jnp.int32)[None, :] * blocks + block_ids[:, None] < npages
     ).reshape(-1)

time: 97.9 us -> 75.9 us (0.78)
  between operations: 14.3 us -> 0.95 us
  waiting for transfers between devices: 45.4 us -> 38.1 us
  starting transfers between devices: 6.32 us -> 10.2 us
  matrix products: 11.7 us -> 8.89 us
  local copies, waits for them, and re-layouts: 9.17 us -> 6.4 us
    all_gather x1 -> x0, waiting for transfers between devices: 21.3 us -> none  [local(): gathered = lax.all_gather(compact, 'blk', axis=0, tiled=True)]
    ppermute x0 -> x3, waiting for transfers between devices: none -> 14.9 us  [the longest x2 12.8 us: local(): lax.ppermute(small, axis_name='blk', perm=[(dd, (dd + 1) % z1) for dd in...]
    ppermute x0 -> x3, starting transfers between devices: none -> 3.87 us  [the longest x1 3.81 us: local(): lax.ppermute(k_now, axis_name='blk', perm=[(dd, (dd - 1) % z1) for dd in...]
    dot_general x2, matrix products: 5.92 us -> 3.1 us  [attend(): jnp.einsum('gqd,gkd->gqk', queries, keys, preferred_element_type=jnp.floa...]
    select_n x1, other arithmetic: 0.7 us -> 2.01 us  [local(): wanted = (block_ids[:, None] - my_start) % blocks + peer_slots * blocks]
    transpose x1 -> x0, local copies, waits for them, and re-layouts: 1.29 us -> none  [local(): gathered.transpose(1, 0, 2, 3)]
  transfers between devices with their start and end apart: 2 -> 4, of which waited for: 2 -> 4; matrix products, arithmetic and copies ran while one was open for 7% -> 4% of each run, Pallas kernels for 0% -> 0%
where the time goes in v1:
time: 75.9 us; the launch traced here: 75.7 us
  waiting for transfers between devices  38.1 us (50%)
  other arithmetic  11.2 us (15%)
  starting transfers between devices  10.2 us (13%)
  matrix products  8.89 us (12%)
  local copies, waits for them, and re-layouts  6.4 us (8%)
  between operations  0.95 us (1%)
    all_to_all x1, waiting for transfers between devices, local(): lax.all_to_all(payload, 'blk', split_axis=0, concat_axis=0, tiled=True)  23.2 us
    ppermute x2, waiting for transfers between devices, local(): lax.ppermute(small, axis_name='blk', perm=[(dd, (dd + 1) % z1) for dd in...  12.8 us
    all_to_all x1, starting transfers between devices, local(): lax.all_to_all(payload, 'blk', split_axis=0, concat_axis=0, tiled=True)  6.32 us
    dot_general x2, matrix products, attend(): jnp.einsum('gqk,gkd->gqd', weights.astype(jnp.bfloat16), values, preferre...  5.79 us
    reduce_sum x2, other arithmetic, attend(): totals = totals * factor + jnp.sum(weights, axis=2)  4.12 us
    ppermute x1, starting transfers between devices, local(): lax.ppermute(k_now, axis_name='blk', perm=[(dd, (dd - 1) % z1) for dd in...  3.81 us
    dot_general x2, matrix products, attend(): jnp.einsum('gqd,gkd->gqk', queries, keys, preferred_element_type=jnp.floa...  3.1 us
    gather x1, local copies, waits for them, and re-layouts, local(): kv_cache[chosen]  2.77 us
  transfers between devices with their start and end apart: 4, of which 4 were waited for; matrix products, arithmetic and copies ran while one was open for 4% of the time, Pallas kernels for 0%

profile of v1, /device:TPU:0, one launch (start us, length us, event | category | flops | bytes accessed | tf_op | source)
XLA Modules:
  0.0 75.7 jit_solution(14516020960253932291)
XLA Ops:
  0.0 0.0 copy-start.1
  0.0 0.0 copy-start
  0.0 0.7 and_select_fusion.3
  0.7 0.7 convert_bitcast_fusion
  1.4 0.2 reduce-window.21
  1.6 0.1 convert_reduce_fusion
  1.7 0.2 reduce-window.22
  1.9 0.6 fusion.36
  2.5 2.0 %and_select_fusion.4 = (s32[4]{0:T(128)S(1)}, s32[]{:T(128)}) fusion(s32[]{:T(128)} %fusion.36, s32[4]{0:T(128)} %param.9, s32[]{:T(128)S(6)} %axis_index.19), kind=kLoop, calls=%fused_computation.71 | loop fusion | flops 59 | bytes 44 | tf_op jit(solution)/shard_map/jit(remainder)/select_n | solution.py:56
  4.5 0.2 select_reduce_fusion.1
  4.7 0.9 %copy.17 = bf16[2,128,256]{2,1,0:T(8,128)(2,1)S(1)} copy(bf16[2,128,256]{2,0,1:T(2,128)(2,1)} %bitcast.101) | data formatting | bytes 262144 | tf_op jit(solution)/shard_map/transpose | solution.py:64
  5.7 2.8 %gather_fusion = bf16[4,2,128,256]{3,2,1,0:T(8,128)(2,1)S(1)} fusion(bf16[32,2,128,256]{3,2,1,0:T(8,128)(2,1)} %param.7, s32[1024]{0:T(1024)S(1)} %pad_clamp_fusion.1), kind=kCustom, calls=%fused_computation | custom fusion | bytes 1048592 | tf_op jit(solution)/shard_map/gather | solution.py:59
  8.5 1.1 %pad_maximum_fusion = bf16[4,2,256,256]{3,2,1,0:T(8,128)(2,1)} fusion(bf16[4,2,128,256]{3,2,1,0:T(8,128)(2,1)S(1)} %broadcast_in_dim.153, bf16[4,2,128,256]{3,2,1,0:T(8,128)(2,1)S(1)} %gather_fusion), kind=kLoop, calls=%fused_computation.23 | loop fusion | flops 2097152 | bytes 2097152 | tf_op jit(solution)/shard_map/concatenate | solution.py:66
  9.5 6.3 %all-to-all-start = ((bf16[4,2,256,256]{3,2,1,0:T(8,128)(2,1)}), bf16[4,2,256,256]{3,2,1,0:T(8,128)(2,1)S(1)}, u32[]{:S(2)}, u32[]{:S(2)}) async-start(bf16[4,2,256,256]{3,2,1,0:T(8,128)(2,1)} %pad_maximum_fusion), calls=%async_computation | async-start | bytes 2097152 | tf_op jit(solution)/shard_map/all_to_all | solution.py:67
  15.9 0.1 broadcast_bitcast_fusion.2
  16.0 0.1 and.112
  16.1 0.2 reduce-window.23
  17.0 0.0 copy-done
  17.0 0.1 copy.30
  17.1 0.1 copy.20
  17.3 0.1 fusion.33
  17.4 0.0 copy-done.1
  17.4 0.1 select_reduce_fusion
  17.5 0.1 broadcast_bitcast_fusion.1
  17.6 0.4 broadcast_compare_fusion
  18.0 0.4 pad_add_fusion
  18.4 23.2 %all-to-all-done = bf16[4,2,256,256]{3,2,1,0:T(8,128)(2,1)S(1)} async-done(((bf16[4,2,256,256]{3,2,1,0:T(8,128)(2,1)}), bf16[4,2,256,256]{3,2,1,0:T(8,128)(2,1)S(1)}, u32[]{:S(2)}, u32[]{:S(2)}) %all-to-all-start) | async-done | bytes 1048608 | tf_op jit(solution)/shard_map/all_to_all | solution.py:67
  41.6 0.1 fusion.51
  41.7 0.6 gather_fusion.1
  42.3 0.1 collective-permute-start
  42.3 3.8 %collective-permute-start.1 = (bf16[2,2,128,256]{3,2,1,0:T(8,128)(2,1)S(1)}, bf16[2,2,128,256]{3,2,1,0:T(8,128)(2,1)S(1)}, u32[]{:S(2)}, u32[]{:S(2)}) collective-permute-start(bf16[2,2,128,256]{3,2,1,0:T(8,128)(2,1)S(1)} %gather_fusion.1), channel_id=1, source_target_pairs={{0,12},{4,0},{8,4},{12,8},{1,13},{5,1},{9,5},{13,9},{2,14},{6,2},{... | collective-permute-start | bytes 786440 | tf_op jit(solution)/shard_map/ppermute | solution.py:94
  46.2 1.4 %fusion.4 = (f32[2,1024]{1,0:T(2,128)S(1)}, f32[2,768,1024]{2,1,0:T(8,128)S(1)}) fusion(pred[1024,768]{0,1:T(8,128)(4,1)S(1)} %pad_add_fusion, bf16[2,1024,128]{2,1,0:T(8,128)(2,1)S(1)} %bitcast.91, bf16[2,512,256]{2,1,0:T(8,128)(2,1)S(1)} %bitcast.96, bf16[2,256,256]{2,1,0:T(8,128)(2,1)S(1)} %bitcast.99), kind=kOutput, calls=%fused_computation.11 | convolution fusion | flops 408156160 | bytes 8396800 | tf_op jit(solution)/shard_map/gqd,gkd->gqk/dot_general | solution.py:14
  47.6 0.1 broadcast_in_dim.162
  47.7 5.6 %collective-permute-done = bf16[2,2,128,256]{3,2,1,0:T(8,128)(2,1)S(1)} collective-permute-done((bf16[2,2,128,256]{3,2,1,0:T(8,128)(2,1)S(1)}, bf16[2,2,128,256]{3,2,1,0:T(8,128)(2,1)S(1)}, u32[]{:S(2)}, u32[]{:S(2)}) %collective-permute-start) | collective-permute-done | bytes 262176 | tf_op jit(solution)/shard_map/ppermute | solution.py:89
  53.4 0.0 collective-permute-start.2
  53.4 2.0 %collective-permute-done.1 = bf16[2,2,128,256]{3,2,1,0:T(8,128)(2,1)S(1)} collective-permute-done((bf16[2,2,128,256]{3,2,1,0:T(8,128)(2,1)S(1)}, bf16[2,2,128,256]{3,2,1,0:T(8,128)(2,1)S(1)}, u32[]{:S(2)}, u32[]{:S(2)}) %collective-permute-start.1) | collective-permute-done | bytes 262176 | tf_op jit(solution)/shard_map/ppermute | solution.py:94
  55.4 7.2 %collective-permute-done.2 = bf16[2,2,128,256]{3,2,1,0:T(8,128)(2,1)S(1)} collective-permute-done((bf16[2,2,128,256]{3,2,1,0:T(8,128)(2,1)S(1)}, bf16[2,2,128,256]{3,2,1,0:T(8,128)(2,1)S(1)}, u32[]{:S(2)}, u32[]{:S(2)}) %collective-permute-start.2) | collective-permute-done | bytes 262176 | tf_op jit(solution)/shard_map/ppermute | solution.py:89
  62.7 1.7 %bitcast_reduce_fusion = (f32[2,1024]{1,0:T(2,128)S(1)}, f32[2,1024,1024]{2,1,0:T(8,128)S(1)}) fusion(pred[1024]{0:T(1024)(128)(4,1)S(1)} %broadcast_bitcast_fusion.1, bf16[2,1024,128]{2,1,0:T(8,128)(2,1)S(1)} %bitcast.92, bf16[2,1024,256]{2,1,0:T(8,128)(2,1)S(1)} %bitcast.88), kind=kOutput, calls=%fused_computation.3 | convolution fusion | flops 543160320 | bytes 9446400 | tf_op jit(solution)/shard_map/gqd,gkd->gqk/dot_general | solution.py:14
  64.4 2.5 %fusion.2 = f32[2,1024]{1,0:T(2,128)S(1)} fusion(f32[2,1024,1024]{2,1,0:T(8,128)S(1)} %get-tuple-element.18, f32[2,1024]{1,0:T(2,128)S(1)} %get-tuple-element.13, pred[1024]{0:T(1024)(128)(4,1)S(1)} %broadcast_bitcast_fusion.1), kind=kLoop, calls=%fused_computation.9 | loop fusion | flops 10483712 | bytes 8406016 | tf_op jit(solution)/shard_map/reduce_sum | solution.py:20
  66.9 1.7 %fusion.5 = f32[2,1024]{1,0:T(2,128)S(1)} fusion(f32[2,768,1024]{2,1,0:T(8,128)S(1)} %get-tuple-element.16, f32[2,1024]{1,0:T(2,128)S(1)} %get-tuple-element.14, pred[1024,768]{0,1:T(8,128)(4,1)S(1)} %pad_add_fusion), kind=kLoop, calls=%fused_computation.12 | loop fusion | flops 7862272 | bytes 7094272 | tf_op jit(solution)/shard_map/reduce_sum | solution.py:20
  68.6 2.8 %fusion.20 = f32[2,1024,128]{2,1,0:T(8,128)S(1)} fusion(f32[2,768,1024]{2,1,0:T(8,128)S(1)} %get-tuple-element.16, f32[2,1024]{1,0:T(2,128)S(1)} %get-tuple-element.14, pred[1024,768]{0,1:T(8,128)(4,1)S(1)} %pad_add_fusion, f32[2,1024]{1,0:T(2,128)S(1)} %get-tuple-element.6, f32[2,1024]{1,0:T(2,128)S(1)} %get-tuple-element.12, ...), kind=kOutput, calls=%fused_computation.22 | convolution fusion | flops 411828224 | bytes 8937472 | tf_op jit(solution)/shard_map/gqk,gkd->gqd/dot_general | solution.py:21
  71.4 3.0 %divide_convert_fusion = bf16[2,1024,128]{2,1,0:T(8,128)(2,1)S(1)} fusion(f32[2,1024,128]{2,1,0:T(8,128)S(1)} %fusion.20, f32[2,1024,1024]{2,1,0:T(8,128)S(1)} %get-tuple-element.18, f32[2,1024]{1,0:T(2,128)S(1)} %get-tuple-element.13, pred[1024]{0:T(1024)(128)(4,1)S(1)} %broadcast_bitcast_fusion.1, bf16[2,1024,256]{2,1,0:T(8,128)(2,1)S(1)} %bitcast.89, ...), kind=kOutput, calls=%fused_computation.24 | convolution fusion | flops 548143104 | bytes 10504192 | tf_op jit(solution)/shard_map/gqk,gkd->gqd/dot_general | solution.py:21
  74.4 0.3 copy.27
  74.7 0.9 %copy.37 = bf16[16,8,16,128]{3,1,2,0:T(8,128)(2,1)} copy(bf16[16,8,16,128]{3,2,1,0:T(8,128)(2,1)S(1)} %bitcast.93) | data formatting | bytes 1048576
  (25 shorter events, 0.3 us)
Async XLA Ops:
  0.0 17.4 %copy-start.1 = (s32[4]{0:T(128)S(1)}, s32[4]{0:T(128)}, u32[]{:S(2)}) copy-start(s32[4]{0:T(128)} %param.9) | copy-start | bytes 52
  0.0 17.0 %copy-start = (bf16[128,2048]{1,0:T(8,128)(2,1)S(1)}, bf16[128,2048]{1,0:T(8,128)(2,1)}, u32[]{:S(2)}) copy-start(bf16[128,2048]{1,0:T(8,128)(2,1)} %param.5) | copy-start | bytes 1572868
  9.5 32.0 %all-to-all-start = ((bf16[4,2,256,256]{3,2,1,0:T(8,128)(2,1)}), bf16[4,2,256,256]{3,2,1,0:T(8,128)(2,1)S(1)}, u32[]{:S(2)}, u32[]{:S(2)}) async-start(bf16[4,2,256,256]{3,2,1,0:T(8,128)(2,1)} %pad_maximum_fusion), calls=%async_computation | async-start | bytes 2097152 | tf_op jit(solution)/shard_map/all_to_all | solution.py:67
  42.3 11.1 %collective-permute-start = (bf16[2,2,128,256]{3,2,1,0:T(8,128)(2,1)S(1)}, bf16[2,2,128,256]{3,2,1,0:T(8,128)(2,1)S(1)}, u32[]{:S(2)}, u32[]{:S(2)}) collective-permute-start(bf16[2,2,128,256]{3,2,1,0:T(8,128)(2,1)S(1)} %gather_fusion.1), channel_id=1, source_target_pairs={{0,4},{4,8},{8,12},{12,0},{1,5},{5,9},{9,13},{13,1},{2,6},{6,10},{... | collective-permute-start | bytes 786440 | tf_op jit(solution)/shard_map/ppermute | solution.py:89
  42.3 13.1 %collective-permute-start.1 = (bf16[2,2,128,256]{3,2,1,0:T(8,128)(2,1)S(1)}, bf16[2,2,128,256]{3,2,1,0:T(8,128)(2,1)S(1)}, u32[]{:S(2)}, u32[]{:S(2)}) collective-permute-start(bf16[2,2,128,256]{3,2,1,0:T(8,128)(2,1)S(1)} %gather_fusion.1), channel_id=1, source_target_pairs={{0,12},{4,0},{8,4},{12,8},{1,13},{5,1},{9,5},{13,9},{2,14},{6,2},{... | collective-permute-start | bytes 786440 | tf_op jit(solution)/shard_map/ppermute | solution.py:94
  53.4 9.3 %collective-permute-start.2 = (bf16[2,2,128,256]{3,2,1,0:T(8,128)(2,1)S(1)}, bf16[2,2,128,256]{3,2,1,0:T(8,128)(2,1)S(1)}, u32[]{:S(2)}, u32[]{:S(2)}) collective-permute-start(bf16[2,2,128,256]{3,2,1,0:T(8,128)(2,1)S(1)} %collective-permute-done), channel_id=1, source_target_pairs={{0,4},{4,8},{8,12},{12,0},{1,5},{5,9},{9,13},{13,1},{2,6},{6,10},{... | collective-permute-start | bytes 786440 | tf_op jit(solution)/shard_map/ppermute | solution.py:89
